TPU v7x, 512 devices: a whole 4x4x16 slice. The times are simulated.
512 devices in a mesh: grp: 4 (over y), seq: 32 (over z, core), mp: 4 (over x).
Axes of the slice: x: 4, y: 4, z: 16, core: 2. Of those that a mesh axis runs over, the one named last changes fastest.
Arguments:
- queries: bfloat16 [4, 4096, 2048], P('grp', 'seq', 'mp'), may hold values from -16 to 16
- d_out: bfloat16 [4, 4096, 2048], P('grp', 'seq', 'mp'), may hold values from -6 to 6
- neighbour_kv: bfloat16 [4, 256, 128, 2, 2048], P('grp', 'seq', None, None, 'mp'), may hold values from -16 to 16
- target: int32 [4, 256], P('grp', 'seq'), may hold values from -1 to 127, as said below
- bias: float32 [16, 191], P('mp'), may hold values from -6 to 6
Outputs:
- attended: bfloat16 [4, 4096, 2048], P('grp', 'seq', 'mp')
- d_query: bfloat16 [4, 4096, 2048], P('grp', 'seq', 'mp')
- d_kv: bfloat16 [4, 256, 128, 2, 2048], P('grp', 'seq', None, None, 'mp')
- d_bias: float32 [16, 191], P('mp')
Inputs may be any that keep to these rules, and one draw needn't show every extreme that they name: `target`: in each group every entry 0..127 stands in exactly one slot and -1 marks an empty slot. The slots of one index of seq hold at most 1 entries e with the same e // 4, and some index reaches that; some index of seq holds 8 entries.
All inputs are finite; a program needn't handle non-finite values.
Results may differ from a plain program's by a relative error of at most 0.011.
Values may be sent and summed in bfloat16 or wider, within the bound.
No kernel may reach another device: no remote copies, remote signals or barrier semaphores. Data moves between devices by JAX's collectives and lax.ppermute only.
A program may use at most 128 MiB of HBM per device.

v0:
```python
import jax
import jax.numpy as jnp
from jax import lax
from jax.sharding import PartitionSpec as P

STRETCH = 64
NB_LEN = 128
SEQ_LEN = 2048


def passed_along(block, axis, distance):
    devices = range(lax.axis_size(axis))
    route = [(i - distance, i) for i in devices if i - distance in devices]
    return lax.ppermute(block, axis, route)


def bias_grid(lookup, row_count, col_count):
    head_num = lookup.shape[0]
    span = row_count + col_count
    padded = jnp.pad(lookup, ((0, 0), (0, 1)))
    flattened = jnp.tile(padded, (1, row_count))
    flattened = jnp.pad(flattened, ((0, 0), (0, row_count)))
    shaped = flattened.reshape(head_num, row_count, span + 1)[:, :, :col_count]
    return shaped[:, :, ::-1]


def bias_fold(grads):
    head_num, row_count, col_count = grads.shape
    turned = grads[:, :, ::-1]
    padded = jnp.pad(turned, ((0, 0), (0, 0), (0, row_count)))
    flattened = padded.reshape(head_num, row_count * (row_count + col_count))
    flattened = flattened[:, : row_count * (row_count + col_count - 1)]
    return jnp.sum(flattened.reshape(head_num, row_count, row_count + col_count - 1), axis=1)


def take_rows(table, index, valid):
    rows = jnp.take(table, index, axis=0)
    shape = (valid.shape[0],) + (1,) * (rows.ndim - 1)
    return jnp.where(valid.reshape(shape), rows, jnp.zeros((), rows.dtype))


def exchange(block):
    return lax.all_to_all(block, "seq", split_axis=0, concat_axis=0, tiled=True)


def local(queries, d_out, neighbour_kv, target, bias):
    tok_rows = queries.shape[1]
    width_dev = queries.shape[2]
    head_count = bias.shape[0]
    head_depth = width_dev // head_count
    stretch_count = tok_rows // STRETCH
    per_owner = 2 * stretch_count
    shard_count = lax.axis_size("seq")
    my_index = lax.axis_index("seq")
    group_rows = tok_rows * shard_count
    seq_stretches = min(SEQ_LEN, group_rows) // STRETCH
    scale_factor = head_depth ** (-0.5)
    bias_rows = bias_grid(bias, STRETCH, NB_LEN).transpose(1, 0, 2)
    row_ids = jnp.arange(STRETCH)
    q_all = lax.all_gather(queries[0], "seq", axis=0, tiled=True)
    g_all = lax.all_gather(d_out[0], "seq", axis=0, tiled=True)
    my_targets = target[0]
    slot_count = my_targets.shape[0]
    is_used = my_targets >= 0
    entry = jnp.where(is_used, my_targets, 0)
    stretch_of = entry // 2
    win_rows = stretch_of[:, None] * STRETCH + (STRETCH - 1) + row_ids[None, :]
    in_group = win_rows < group_rows
    win_rows = jnp.minimum(win_rows.reshape(-1), group_rows - 1)
    q_win = jnp.take(q_all, win_rows, axis=0).reshape(slot_count, STRETCH, width_dev)
    g_win = jnp.take(g_all, win_rows, axis=0).reshape(slot_count, STRETCH, width_dev)
    live_slot = (row_ids[None, :] == 0) | ((stretch_of[:, None] + 1) % seq_stretches != 0)
    q_keep = is_used[:, None] & in_group
    q_slots = jnp.where(q_keep[:, :, None], q_win, jnp.zeros((), q_win.dtype))
    g_slots = jnp.where((q_keep & live_slot)[:, :, None], g_win, jnp.zeros((), g_win.dtype))
    q_slots = q_slots.reshape(slot_count, STRETCH, head_count, head_depth)
    g_slots = g_slots.reshape(slot_count, STRETCH, head_count, head_depth)
    stored = neighbour_kv[0]
    key_rows = stored[:, :, 0].reshape(slot_count, NB_LEN, head_count, head_depth)
    value_rows = stored[:, :, 1].reshape(slot_count, NB_LEN, head_count, head_depth)
    scores = jnp.einsum("sihd,sjhd->sihj", q_slots, key_rows, preferred_element_type=jnp.float32)
    scores = scores * scale_factor + bias_rows[None]
    peak_val = jnp.max(scores, axis=-1)
    weights = jnp.exp(scores - peak_val[..., None])
    row_total = jnp.sum(weights, axis=-1)
    partial_value = jnp.einsum(
        "sihj,sjhd->sihd",
        weights.astype(jnp.bfloat16),
        value_rows,
        preferred_element_type=jnp.float32,
    )
    owner_of = jnp.where(is_used, my_targets // per_owner, -1)
    owner_match = owner_of[None, :] == jnp.arange(shard_count)[:, None]
    send_slot = jnp.argmax(owner_match, axis=1)
    send_has = jnp.any(owner_match, axis=1)
    part_send = take_rows(
        partial_value.astype(jnp.bfloat16).reshape(slot_count, STRETCH, width_dev),
        send_slot,
        send_has,
    )
    slot_stats = jnp.concatenate(
        [
            jnp.stack([peak_val, row_total], axis=1).reshape(slot_count, -1),
            (entry + 1).astype(jnp.float32)[:, None],
        ],
        axis=1,
    )
    stat_send = take_rows(slot_stats, send_slot, send_has)
    part_recv = exchange(part_send)
    stat_recv = exchange(stat_send)
    own_entries = my_index * per_owner + jnp.arange(per_owner)
    sent_ids = stat_recv[:, -1].astype(jnp.int32) - 1
    where_held = sent_ids[None, :] == own_entries[:, None]
    held_by = jnp.argmax(where_held, axis=1)
    parts_own = jnp.take(part_recv, held_by, axis=0).astype(jnp.float32)
    parts_own = parts_own.reshape(stretch_count, 2, STRETCH, head_count, head_depth)
    stats_own = jnp.take(stat_recv[:, :-1], held_by, axis=0)
    stats_own = stats_own.reshape(stretch_count, 2, 2, STRETCH, head_count)
    peaks_own = stats_own[:, :, 0]
    totals_own = stats_own[:, :, 1]
    stretch_ids = my_index * stretch_count + jnp.arange(stretch_count)
    is_live = (row_ids[None, :] == 0) | ((stretch_ids[:, None] + 1) % seq_stretches != 0)
    live_rows = is_live.astype(jnp.float32)
    top_peak = jnp.max(peaks_own, axis=1)
    factor = jnp.exp(peaks_own - top_peak[:, None])
    denominator = jnp.sum(factor * totals_own, axis=1)
    combined = jnp.sum(factor[..., None] * parts_own, axis=1) / denominator[..., None]
    combined = combined * live_rows[:, :, None, None]
    att_win = combined.astype(jnp.bfloat16).reshape(tok_rows, width_dev)
    att_before = passed_along(att_win[tok_rows - STRETCH :], "seq", 1)
    g_dot = jnp.einsum(
        "sihd,sihd->sih",
        g_slots.astype(jnp.float32),
        partial_value,
        precision=lax.Precision.HIGHEST,
    )
    mine = jnp.stack([peak_val, row_total, g_dot], axis=1)
    shared = jnp.concatenate(
        [
            mine.reshape(slot_count, -1),
            jnp.where(is_used, entry + 1, 0).astype(jnp.float32)[:, None],
        ],
        axis=1,
    )
    shared_all = lax.all_gather(shared, "seq", tiled=True)
    partner = entry + 1 - 2 * (entry % 2)
    partner_at = jnp.argmax(
        shared_all[None, :, -1] == (partner + 1).astype(jnp.float32)[:, None], axis=1
    )
    theirs = jnp.take(shared_all[:, :-1], partner_at, axis=0).reshape(mine.shape)
    both_peak = jnp.maximum(mine[:, 0], theirs[:, 0])
    mine_f = jnp.exp(mine[:, 0] - both_peak)
    theirs_f = jnp.exp(theirs[:, 0] - both_peak)
    both_total = mine_f * mine[:, 1] + theirs_f * theirs[:, 1]
    lse_slots = both_peak + jnp.log(both_total)
    dd_slots = (mine_f * mine[:, 2] + theirs_f * theirs[:, 2]) / both_total
    dd_slots = jnp.where(is_used[:, None, None], dd_slots, 0.0)
    prob_full = jnp.exp(scores - lse_slots[..., None])
    prob_low = prob_full.astype(jnp.bfloat16)
    grad_prob = jnp.einsum(
        "sihd,sjhd->sihj", g_slots, value_rows, preferred_element_type=jnp.float32
    )
    grad_scores = prob_full * (grad_prob - dd_slots[..., None])
    scores_low = grad_scores.astype(jnp.bfloat16)
    grad_rows = (
        jnp.einsum("sihj,sjhd->sihd", scores_low, key_rows, preferred_element_type=jnp.float32)
        * scale_factor
    )
    mix_probs = jnp.stack([scores_low, prob_low], axis=1)
    mix_rows = jnp.stack([q_slots, g_slots], axis=1)
    grad_kv = jnp.einsum(
        "sxihj,sxihd->sjxhd", mix_probs, mix_rows, preferred_element_type=jnp.float32
    )
    kv_scale = jnp.array([scale_factor, 1.0], jnp.float32)[None, None, :, None, None]
    d_kv = (grad_kv * kv_scale).astype(jnp.bfloat16).reshape(slot_count, NB_LEN, 2, width_dev)
    bias_part = bias_fold(jnp.sum(grad_scores, axis=0).transpose(1, 0, 2))
    dq_rows = jnp.zeros((shard_count, stretch_count, STRETCH, width_dev), jnp.bfloat16)
    dq_owner = jnp.where(is_used, owner_of, shard_count)
    dq_rows = dq_rows.at[dq_owner, stretch_of % stretch_count].set(
        grad_rows.astype(jnp.bfloat16).reshape(slot_count, STRETCH, width_dev), mode="drop"
    )
    grad_win = lax.psum_scatter(dq_rows, "seq", scatter_dimension=0, tiled=True)
    grad_win = grad_win.reshape(tok_rows, width_dev)
    grad_before = passed_along(grad_win[tok_rows - STRETCH :], "seq", 1)
    attended = jnp.concatenate([att_before[1:], att_win[: tok_rows - STRETCH + 1]])
    d_query = jnp.concatenate([grad_before[1:], grad_win[: tok_rows - STRETCH + 1]])
    raw_sum = lax.psum(lax.psum(bias_part, "seq"), "grp")
    squares = lax.psum(jnp.sum(raw_sum * raw_sum), "mp")
    d_bias = raw_sum * jnp.minimum(1.0, 1.0 / jnp.sqrt(squares + 1e-12))
    return (attended[None], d_query[None], d_kv[None], d_bias)


def solution(mesh):
    in_specs = (
        P("grp", "seq", "mp"),
        P("grp", "seq", "mp"),
        P("grp", "seq", None, None, "mp"),
        P("grp", "seq"),
        P("mp", None),
    )
    out_specs = (
        P("grp", "seq", "mp"),
        P("grp", "seq", "mp"),
        P("grp", "seq", None, None, "mp"),
        P("mp", None),
    )
    return jax.shard_map(local, mesh=mesh, in_specs=in_specs, out_specs=out_specs, check_vma=False)
```

profile of v0, /device:TPU:97, one launch (start us, length us, event | category | flops | bytes accessed | tf_op | source)
XLA Modules:
  0.0 430.7 jit_solution(3914705341878619618)
XLA Ops:
  7.2 0.7 all-gather.7.cloned.1.call-update
  8.0 0.7 all-gather.5.cloned.1.call-update
  8.7 0.7 fusion.50
  9.5 0.7 copy.86
  10.2 0.7 pad.12
  11.6 3.8 copy.83
  16.4 2.8 fusion.60
  19.2 67.8 %all-gather.7.cloned.1.call-done = bf16[1,4096,512]{2,1,0:T(8,128)(2,1)} async-done(((bf16[1,128,512]{2,1,0:T(8,128)(2,1)}), bf16[1,4096,512]{2,1,0:T(8,128)(2,1)}) %all-gather.7.cloned.1.call-update) | async-done | bytes 4194320 | tf_op jit(solution)/shard_map/all_gather | solution.py:61
  86.9 4.7 %gather_fusion.6 = bf16[512,512]{1,0:T(8,128)(2,1)S(1)} fusion(bf16[4096,512]{1,0:T(8,128)(2,1)} %bitcast.151, s32[1024]{0:T(1024)S(1)} %pad_clamp_fusion.3), kind=kCustom, calls=%fused_computation.1.clone | custom fusion | bytes 1050624 | tf_op jit(solution)/shard_map/jit(_take)/gather | solution.py:71
  91.7 68.3 %all-gather.5.cloned.1.call-done = bf16[1,4096,512]{2,1,0:T(8,128)(2,1)} async-done(((bf16[1,128,512]{2,1,0:T(8,128)(2,1)}), bf16[1,4096,512]{2,1,0:T(8,128)(2,1)}) %all-gather.5.cloned.1.call-update) | async-done | bytes 4194320 | tf_op jit(solution)/shard_map/all_gather | solution.py:60
  160.0 4.7 %gather_fusion.5 = bf16[512,512]{1,0:T(8,128)(2,1)S(1)} fusion(bf16[4096,512]{1,0:T(8,128)(2,1)} %bitcast.152, s32[1024]{0:T(1024)S(1)} %pad_clamp_fusion.3), kind=kCustom, calls=%fused_computation.clone | custom fusion | bytes 1050624 | tf_op jit(solution)/shard_map/jit(_take)/gather | solution.py:70
  164.9 1.0 reshape.666
  165.8 0.9 reshape.662
  166.8 1.7 fusion.62
  168.5 3.2 fusion.9
  172.1 29.3 %all_gather.11 = f32[256,769]{1,0:T(8,128)S(1)} all-gather(f32[8,769]{1,0:T(8,128)S(1)} %pad_maximum_fusion.3), channel_id=1, replica_groups=mesh['grp'=4,'seq'=32,'mp'=4] {'seq'}, dimensions={0}, use_global_device_ids=true | all-gather | bytes 812064 | tf_op jit(solution)/shard_map/all_gather | solution.py:145
  201.5 0.7 iota_reduce_fusion
  202.3 1.1 copy.142
  203.7 0.6 gather_fusion
  204.4 0.7 copy.89
  205.2 10.6 %all-to-all-start = ((f32[32,1,513]{2,1,0:T(1,128)}), f32[32,1,513]{2,1,0:T(1,128)S(1)}, u32[]{:S(2)}, u32[]{:S(2)}) async-start(f32[32,1,513]{2,1,0:T(1,128)} %copy.89), calls=%async_computation | async-start | bytes 163840 | tf_op jit(solution)/shard_map/all_to_all | solution.py:43
  215.7 2.0 gather_fusion.2
  217.7 3.3 select_select_fusion
  221.1 0.9 slice.114
  222.0 1.7 gather_fusion.4
  224.2 3.4 all-to-all-done
  227.6 8.9 %all-to-all-start.1 = ((bf16[32,64,512]{2,1,0:T(8,128)(2,1)}), bf16[32,64,512]{2,1,0:T(8,128)(2,1)}, u32[]{:S(2)}, u32[]{:S(2)}) async-start(bf16[32,64,512]{2,1,0:T(8,128)(2,1)} %select_select_fusion), calls=%async_computation.1 | async-start | bytes 4194304 | tf_op jit(solution)/shard_map/all_to_all | solution.py:43
  236.7 1.9 fusion.3
  238.6 0.8 fusion.5
  239.7 2.4 broadcast_in_dim.191
  242.1 2.5 scatter_fusion
  245.0 0.8 copy-done.1
  245.8 0.9 fusion.61
  247.4 127.2 %psum.21 = f32[4,191]{1,0:T(4,128)S(1)} all-reduce(f32[4,191]{1,0:T(4,128)S(1)} %reduce_sum.58), channel_id=1, replica_groups=mesh['grp'=4,'seq'=32,'mp'=4] {'seq'}, use_global_device_ids=true, to_apply=%region_13.15 | all-reduce | flops 764 | bytes 6112 | tf_op jit(solution)/shard_map/psum | solution.py:187
  374.6 8.4 %psum.22 = f32[4,191]{1,0:T(4,128)S(1)} all-reduce(f32[4,191]{1,0:T(4,128)S(1)} %psum.21), channel_id=1, replica_groups=mesh['grp'=4,'seq'=32,'mp'=4] {'grp'}, use_global_device_ids=true, to_apply=%region_14.16 | all-reduce | flops 764 | bytes 6112 | tf_op jit(solution)/shard_map/psum | solution.py:187
  383.0 0.6 multiply_reduce_fusion.1
  383.6 9.3 %psum.23 = f32[]{:T(128)} all-reduce(f32[]{:T(128)} %multiply_reduce_fusion.1), channel_id=1, replica_groups=mesh['grp'=4,'seq'=32,'mp'=4] {'mp'}, use_global_device_ids=true, to_apply=%region_16.18 | all-reduce | flops 1 | bytes 8 | tf_op jit(solution)/shard_map/psum | solution.py:188
  394.6 0.9 multiply_convert_fusion
  395.4 3.8 copy.108
  399.9 0.7 iota_reduce_fusion.2
  401.7 2.2 gather_fusion.3
  404.8 9.4 %collective-permute-start = (bf16[64,512]{1,0:T(8,128)(2,1)S(1)}, bf16[64,512]{1,0:T(8,128)(2,1)S(1)}, u32[]{:S(2)}, u32[]{:S(2)}) collective-permute-start(bf16[64,512]{1,0:T(8,128)(2,1)S(1)} %bitcast.173), channel_id=1, source_target_pairs={{0,4},{4,8},{8,12},{12,16},{16,20},{20,24},{24,28},{28,32},{32,36}... | collective-permute-start | bytes 196616 | tf_op jit(solution)/shard_map/ppermute | solution.py:14
  414.3 1.2 collective-permute-done
  415.6 0.8 slice_bitcast_fusion.1
  416.4 5.5 %collective-permute-start.1 = (bf16[64,512]{1,0:T(8,128)(2,1)S(1)}, bf16[64,512]{1,0:T(8,128)(2,1)S(1)}, u32[]{:S(2)}, u32[]{:S(2)}) collective-permute-start(bf16[64,512]{1,0:T(8,128)(2,1)S(1)} %slice_bitcast_fusion.1), channel_id=1, source_target_pairs={{0,4},{4,8},{8,12},{12,16},{16,20},{20,24},{24,28},{28,32},{32,36}... | collective-permute-start | bytes 196616 | tf_op jit(solution)/shard_map/ppermute | solution.py:14
  421.9 0.7 maximum_bitcast_fusion
  422.6 0.9 slice.120
  423.5 0.7 maximum_bitcast_fusion.1
  (111 shorter events, 8.3 us)
Async XLA Ops:
  7.2 4.4 %copy-start.6 = (bf16[1,8,128,2,512]{4,3,2,1,0:T(2,128)(2,1)S(1)}, bf16[1,8,128,2,512]{4,3,2,1,0:T(2,128)(2,1)}, u32[]{:S(2)}) copy-start(bf16[1,8,128,2,512]{4,3,2,1,0:T(2,128)(2,1)} %param.10) | copy-start | bytes 6291460
  7.2 79.8 %all-gather.7.cloned.1.call-start = ((), (), s32[]{:S(2)}) async-start(), calls=%async_computation.5 | async-start | bytes 4325376 | tf_op jit(solution)/shard_map/all_gather | solution.py:61
  7.9 152.1 %all-gather.5.cloned.1.call-start = ((), (), s32[]{:S(2)}) async-start(), calls=%async_computation.4 | async-start | bytes 4325376 | tf_op jit(solution)/shard_map/all_gather | solution.py:60
  11.6 3.8 copy-start.10
  164.9 3.6 copy-start.2
  166.8 1.7 copy-start.7
  201.4 0.9 copy-start.4
  205.2 22.5 %all-to-all-start = ((f32[32,1,513]{2,1,0:T(1,128)}), f32[32,1,513]{2,1,0:T(1,128)S(1)}, u32[]{:S(2)}, u32[]{:S(2)}) async-start(f32[32,1,513]{2,1,0:T(1,128)} %copy.89), calls=%async_computation | async-start | bytes 163840 | tf_op jit(solution)/shard_map/all_to_all | solution.py:43
  217.7 3.4 copy-start.5
  224.2 12.5 %copy-start.8 = (bf16[8,64,4,128]{3,2,1,0:T(4,128)(2,1)S(1)}, bf16[8,64,4,128]{3,2,1,0:T(4,128)(2,1)}, u32[]{:S(2)}) copy-start(bf16[8,64,4,128]{3,2,1,0:T(4,128)(2,1)} %reshape.666) | copy-start | bytes 1572868
  227.6 174.1 %all-to-all-start.1 = ((bf16[32,64,512]{2,1,0:T(8,128)(2,1)}), bf16[32,64,512]{2,1,0:T(8,128)(2,1)}, u32[]{:S(2)}, u32[]{:S(2)}) async-start(bf16[32,64,512]{2,1,0:T(8,128)(2,1)} %select_select_fusion), calls=%async_computation.1 | async-start | bytes 4194304 | tf_op jit(solution)/shard_map/all_to_all | solution.py:43
  236.6 179.0 %reduce-scatter.2.cloned.1.call-start = ((), (), s32[]{:S(2)}) async-start(), calls=%async_computation.3 | async-start | bytes 4325376 | tf_op jit(solution)/shard_map/reduce_scatter | solution.py:182
  238.6 1.0 copy-start
  244.6 1.2 copy-start.1
  244.6 148.3 %copy-start.3 = (bf16[512,512]{1,0:T(8,128)(2,1)S(1)}, bf16[512,512]{1,0:T(8,128)(2,1)}, u32[]{:S(2)}) copy-start(bf16[512,512]{1,0:T(8,128)(2,1)} %copy-done.2) | copy-start | bytes 1572868
  393.2 1.3 copy-start.9
  393.2 1.3 copy-start.11
  404.8 10.7 %collective-permute-start = (bf16[64,512]{1,0:T(8,128)(2,1)S(1)}, bf16[64,512]{1,0:T(8,128)(2,1)S(1)}, u32[]{:S(2)}, u32[]{:S(2)}) collective-permute-start(bf16[64,512]{1,0:T(8,128)(2,1)S(1)} %bitcast.173), channel_id=1, source_target_pairs={{0,4},{4,8},{8,12},{12,16},{16,20},{20,24},{24,28},{28,32},{32,36}... | collective-permute-start | bytes 196616 | tf_op jit(solution)/shard_map/ppermute | solution.py:14
  416.4 7.0 %collective-permute-start.1 = (bf16[64,512]{1,0:T(8,128)(2,1)S(1)}, bf16[64,512]{1,0:T(8,128)(2,1)S(1)}, u32[]{:S(2)}, u32[]{:S(2)}) collective-permute-start(bf16[64,512]{1,0:T(8,128)(2,1)S(1)} %slice_bitcast_fusion.1), channel_id=1, source_target_pairs={{0,4},{4,8},{8,12},{12,16},{16,20},{20,24},{24,28},{28,32},{32,36}... | collective-permute-start | bytes 196616 | tf_op jit(solution)/shard_map/ppermute | solution.py:14
Sparse Core Ops, SparseCore 0:
  10.1 76.7 all-gather.6
  89.1 70.8 all-gather.4
  244.8 153.5 reduce-scatter.1
where the time goes:
time: 432 us; the launch traced here: 431 us
  blocking collectives  174 us (40%)
  waiting for transfers between devices  142 us (33%)
  local copies, waits for them, and re-layouts  44 us (10%)
  starting transfers between devices  34.5 us (8%)
  between operations  15 us (3%)
  other arithmetic  12.3 us (3%)
  matrix products  8.49 us (2%)
    psum x2, blocking collectives, local(): raw_sum = lax.psum(lax.psum(bias_part, 'seq'), 'grp')  136 us
    all_gather x1, waiting for transfers between devices, local(): q_all = lax.all_gather(queries[0], 'seq', axis=0, tiled=True)  68.3 us
    all_gather x1, waiting for transfers between devices, local(): g_all = lax.all_gather(d_out[0], 'seq', axis=0, tiled=True)  67.8 us
    all_gather x1, blocking collectives, local(): shared_all = lax.all_gather(shared, 'seq', tiled=True)  29.3 us
    all_to_all x2, starting transfers between devices, exchange(): return lax.all_to_all(block, 'seq', split_axis=0, concat_axis=0, tiled=True)  19.5 us
    ppermute x2, starting transfers between devices, passed_along(): return lax.ppermute(block, axis, route)  14.9 us
    psum x1, blocking collectives, local(): squares = lax.psum(jnp.sum(raw_sum * raw_sum), 'mp')  9.29 us
    unnamed x29, local copies, waits for them, and re-layouts  8.74 us
  transfers between devices with their start and end apart: 7, of which 4 were waited for; matrix products, arithmetic and copies ran while one was open for 11% of the time, Pallas kernels for 0%

commit v1 on v0

--- a/solution.py
+++ b/solution.py
@@ -6,6 +6,11 @@
 STRETCH = 64
 NB_LEN = 128
 SEQ_LEN = 2048
+
+
+def all_by_exchange(x, name, along):
+    outgoing = jnp.stack([x] * lax.axis_size(name))
+    return jnp.concatenate(lax.all_to_all(outgoing, name, 0, 0), axis=along)
 
 
 def passed_along(block, axis, distance):
@@ -57,7 +62,7 @@
     scale_factor = head_depth ** (-0.5)
     bias_rows = bias_grid(bias, STRETCH, NB_LEN).transpose(1, 0, 2)
     row_ids = jnp.arange(STRETCH)
-    q_all = lax.all_gather(queries[0], "seq", axis=0, tiled=True)
+    q_all = all_by_exchange(queries[0], "seq", 0)
     g_all = lax.all_gather(d_out[0], "seq", axis=0, tiled=True)
     my_targets = target[0]
     slot_count = my_targets.shape[0]

time: 432 us -> 505 us (1.17)
  waiting for transfers between devices: 142 us -> 197 us
  starting transfers between devices: 34.5 us -> 47.9 us
    all_gather x1, waiting for transfers between devices: 67.8 us -> 146 us  [local(): g_all = lax.all_gather(d_out[0], 'seq', axis=0, tiled=True)]
    all_gather x1 -> x0, waiting for transfers between devices: 68.3 us -> none  [local(): q_all = lax.all_gather(queries[0], 'seq', axis=0, tiled=True)]
    all_to_all x0 -> x1, waiting for transfers between devices: none -> 45.4 us  [all_by_exchange(): return jnp.concatenate(lax.all_to_all(outgoing, name, 0, 0), axis=along)]
    all_to_all x0 -> x1, starting transfers between devices: none -> 14.9 us  [all_by_exchange(): return jnp.concatenate(lax.all_to_all(outgoing, name, 0, 0), axis=along)]
  transfers between devices with their start and end apart: 7 -> 7, of which waited for: 4 -> 4; matrix products, arithmetic and copies ran while one was open for 11% -> 9% of each run, Pallas kernels for 0% -> 0%
where the time goes in v1:
time: 505 us; the launch traced here: 504 us
  waiting for transfers between devices  197 us (39%)
  blocking collectives  177 us (35%)
  starting transfers between devices  47.9 us (9%)
  local copies, waits for them, and re-layouts  46.1 us (9%)
  between operations  15.3 us (3%)
  other arithmetic  11.6 us (2%)
  matrix products  8.49 us (2%)
    all_gather x1, waiting for transfers between devices, local(): g_all = lax.all_gather(d_out[0], 'seq', axis=0, tiled=True)  146 us
    psum x2, blocking collectives, local(): raw_sum = lax.psum(lax.psum(bias_part, 'seq'), 'grp')  136 us
    all_to_all x1, waiting for transfers between devices, all_by_exchange(): return jnp.concatenate(lax.all_to_all(outgoing, name, 0, 0), axis=along)  45.4 us
    all_gather x1, blocking collectives, local(): shared_all = lax.all_gather(shared, 'seq', tiled=True)  32.3 us
    all_to_all x2, starting transfers between devices, exchange(): return lax.all_to_all(block, 'seq', split_axis=0, concat_axis=0, tiled=True)  17.8 us
    all_to_all x1, starting transfers between devices, all_by_exchange(): return jnp.concatenate(lax.all_to_all(outgoing, name, 0, 0), axis=along)  14.9 us
    ppermute x2, starting transfers between devices, passed_along(): return lax.ppermute(block, axis, route)  14.9 us
  transfers between devices with their start and end apart: 7, of which 4 were waited for; matrix products, arithmetic and copies ran while one was open for 9% of the time, Pallas kernels for 0%

profile of v1, /device:TPU:97, one launch (start us, length us, event | category | flops | bytes accessed | tf_op | source)
XLA Modules:
  0.0 503.8 jit_solution(7822233720700263543)
XLA Ops:
  7.2 3.3 stack.32
  10.5 14.9 %all-to-all-start = ((bf16[32,128,512]{2,1,0:T(8,128)(2,1)}), bf16[32,128,512]{2,1,0:T(8,128)(2,1)}, u32[]{:S(2)}, u32[]{:S(2)}) async-start(bf16[32,128,512]{2,1,0:T(8,128)(2,1)} %stack.32), calls=%async_computation | async-start | bytes 8388608 | tf_op jit(solution)/shard_map/all_to_all | solution.py:13
  25.5 0.7 all-gather.3.cloned.1.call-update
  27.2 3.8 copy.83
  31.0 0.6 iota_reduce_fusion.1
  32.0 2.8 fusion.60
  34.7 146.4 %all-gather.3.cloned.1.call-done = bf16[1,4096,512]{2,1,0:T(8,128)(2,1)} async-done(((bf16[1,128,512]{2,1,0:T(8,128)(2,1)}), bf16[1,4096,512]{2,1,0:T(8,128)(2,1)}) %all-gather.3.cloned.1.call-update) | async-done | bytes 4194320 | tf_op jit(solution)/shard_map/all_gather | solution.py:66
  181.1 4.7 gather_fusion.6
  185.8 45.4 %all-to-all-done = bf16[32,128,512]{2,1,0:T(8,128)(2,1)} async-done(((bf16[32,128,512]{2,1,0:T(8,128)(2,1)}), bf16[32,128,512]{2,1,0:T(8,128)(2,1)}, u32[]{:S(2)}, u32[]{:S(2)}) %all-to-all-start) | async-done | bytes 4194336 | tf_op jit(solution)/shard_map/all_to_all | solution.py:13
  231.2 4.7 gather_fusion.5
  236.1 1.0 reshape.671
  237.0 0.9 reshape.667
  238.0 1.7 fusion.62
  239.7 3.2 fusion.9
  243.3 32.3 %all_gather.7 = f32[256,769]{1,0:T(8,128)S(1)} all-gather(f32[8,769]{1,0:T(8,128)S(1)} %pad_maximum_fusion.3), channel_id=1, replica_groups=mesh['grp'=4,'seq'=32,'mp'=4] {'seq'}, dimensions={0}, use_global_device_ids=true | all-gather | bytes 812064 | tf_op jit(solution)/shard_map/all_gather | solution.py:150
  275.7 0.7 iota_reduce_fusion
  276.5 1.1 copy.142
  277.9 0.6 gather_fusion
  278.7 0.7 copy.89
  279.4 8.8 %all-to-all-start.1 = ((f32[32,1,513]{2,1,0:T(1,128)}), f32[32,1,513]{2,1,0:T(1,128)S(1)}, u32[]{:S(2)}, u32[]{:S(2)}) async-start(f32[32,1,513]{2,1,0:T(1,128)} %copy.89), calls=%async_computation.1 | async-start | bytes 163840 | tf_op jit(solution)/shard_map/all_to_all | solution.py:48
  288.2 2.0 gather_fusion.2
  290.2 3.3 select_select_fusion
  293.6 0.9 slice.114
  294.5 1.7 gather_fusion.4
  296.6 3.4 all-to-all-done.1
  300.1 8.9 %all-to-all-start.2 = ((bf16[32,64,512]{2,1,0:T(8,128)(2,1)}), bf16[32,64,512]{2,1,0:T(8,128)(2,1)}, u32[]{:S(2)}, u32[]{:S(2)}) async-start(bf16[32,64,512]{2,1,0:T(8,128)(2,1)} %select_select_fusion), calls=%async_computation.2 | async-start | bytes 4194304 | tf_op jit(solution)/shard_map/all_to_all | solution.py:48
  309.3 1.9 fusion.3
  311.3 0.8 fusion.5
  312.3 2.4 broadcast_in_dim.191
  314.8 2.5 scatter_fusion
  317.7 0.8 copy-done.1
  318.5 0.9 fusion.61
  320.0 127.2 %psum.21 = f32[4,191]{1,0:T(4,128)S(1)} all-reduce(f32[4,191]{1,0:T(4,128)S(1)} %reduce_sum.58), channel_id=1, replica_groups=mesh['grp'=4,'seq'=32,'mp'=4] {'seq'}, use_global_device_ids=true, to_apply=%region_13.15 | all-reduce | flops 764 | bytes 6112 | tf_op jit(solution)/shard_map/psum | solution.py:192
  447.2 8.8 %psum.22 = f32[4,191]{1,0:T(4,128)S(1)} all-reduce(f32[4,191]{1,0:T(4,128)S(1)} %psum.21), channel_id=1, replica_groups=mesh['grp'=4,'seq'=32,'mp'=4] {'grp'}, use_global_device_ids=true, to_apply=%region_14.16 | all-reduce | flops 764 | bytes 6112 | tf_op jit(solution)/shard_map/psum | solution.py:192
  456.0 0.6 multiply_reduce_fusion.1
  456.6 9.1 %psum.23 = f32[]{:T(128)} all-reduce(f32[]{:T(128)} %multiply_reduce_fusion.1), channel_id=1, replica_groups=mesh['grp'=4,'seq'=32,'mp'=4] {'mp'}, use_global_device_ids=true, to_apply=%region_16.18 | all-reduce | flops 1 | bytes 8 | tf_op jit(solution)/shard_map/psum | solution.py:193
  467.3 0.9 multiply_convert_fusion
  468.1 3.8 copy.108
  471.9 0.6 broadcast_multiply_fusion
  472.6 0.7 iota_reduce_fusion.2
  474.5 2.2 gather_fusion.3
  477.5 9.4 %collective-permute-start = (bf16[64,512]{1,0:T(8,128)(2,1)S(1)}, bf16[64,512]{1,0:T(8,128)(2,1)S(1)}, u32[]{:S(2)}, u32[]{:S(2)}) collective-permute-start(bf16[64,512]{1,0:T(8,128)(2,1)S(1)} %bitcast.174), channel_id=1, source_target_pairs={{0,4},{4,8},{8,12},{12,16},{16,20},{20,24},{24,28},{28,32},{32,36}... | collective-permute-start | bytes 196616 | tf_op jit(solution)/shard_map/ppermute | solution.py:19
  487.1 1.2 collective-permute-done
  488.3 0.8 slice_bitcast_fusion.1
  489.2 5.5 %collective-permute-start.1 = (bf16[64,512]{1,0:T(8,128)(2,1)S(1)}, bf16[64,512]{1,0:T(8,128)(2,1)S(1)}, u32[]{:S(2)}, u32[]{:S(2)}) collective-permute-start(bf16[64,512]{1,0:T(8,128)(2,1)S(1)} %slice_bitcast_fusion.1), channel_id=1, source_target_pairs={{0,4},{4,8},{8,12},{12,16},{16,20},{20,24},{24,28},{28,32},{32,36}... | collective-permute-start | bytes 196616 | tf_op jit(solution)/shard_map/ppermute | solution.py:19
  494.6 0.7 maximum_bitcast_fusion
  495.3 0.9 slice.120
  496.2 0.7 maximum_bitcast_fusion.1
  (113 shorter events, 7.3 us)
Async XLA Ops:
  10.5 15.7 %copy-start.11 = (s32[1,8]{1,0:T(1,128)S(1)}, s32[1,8]{1,0:T(1,128)}, u32[]{:S(2)}) copy-start(s32[1,8]{1,0:T(1,128)} %param.11) | copy-start | bytes 100
  10.5 16.0 %copy-start.10 = (f32[4,191]{1,0:T(4,128)S(1)}, f32[4,191]{1,0:T(4,128)}, u32[]{:S(2)}) copy-start(f32[4,191]{1,0:T(4,128)} %param.12) | copy-start | bytes 9172
  10.5 220.6 %all-to-all-start = ((bf16[32,128,512]{2,1,0:T(8,128)(2,1)}), bf16[32,128,512]{2,1,0:T(8,128)(2,1)}, u32[]{:S(2)}, u32[]{:S(2)}) async-start(bf16[32,128,512]{2,1,0:T(8,128)(2,1)} %stack.32), calls=%async_computation | async-start | bytes 8388608 | tf_op jit(solution)/shard_map/all_to_all | solution.py:13
  25.5 1.7 copy-start.6
  25.5 155.6 %all-gather.3.cloned.1.call-start = ((), (), s32[]{:S(2)}) async-start(), calls=%async_computation.5 | async-start | bytes 4325376 | tf_op jit(solution)/shard_map/all_gather | solution.py:66
  236.0 3.6 copy-start.2
  238.0 1.7 copy-start.7
  275.6 0.9 copy-start.4
  279.4 20.7 %all-to-all-start.1 = ((f32[32,1,513]{2,1,0:T(1,128)}), f32[32,1,513]{2,1,0:T(1,128)S(1)}, u32[]{:S(2)}, u32[]{:S(2)}) async-start(f32[32,1,513]{2,1,0:T(1,128)} %copy.89), calls=%async_computation.1 | async-start | bytes 163840 | tf_op jit(solution)/shard_map/all_to_all | solution.py:48
  290.2 3.4 copy-start.5
  296.6 12.7 %copy-start.8 = (bf16[8,64,4,128]{3,2,1,0:T(4,128)(2,1)S(1)}, bf16[8,64,4,128]{3,2,1,0:T(4,128)(2,1)}, u32[]{:S(2)}) copy-start(bf16[8,64,4,128]{3,2,1,0:T(4,128)(2,1)} %reshape.671) | copy-start | bytes 1572868
  300.1 174.4 %all-to-all-start.2 = ((bf16[32,64,512]{2,1,0:T(8,128)(2,1)}), bf16[32,64,512]{2,1,0:T(8,128)(2,1)}, u32[]{:S(2)}, u32[]{:S(2)}) async-start(bf16[32,64,512]{2,1,0:T(8,128)(2,1)} %select_select_fusion), calls=%async_computation.2 | async-start | bytes 4194304 | tf_op jit(solution)/shard_map/all_to_all | solution.py:48
  309.0 179.3 %reduce-scatter.2.cloned.1.call-start = ((), (), s32[]{:S(2)}) async-start(), calls=%async_computation.4 | async-start | bytes 4325376 | tf_op jit(solution)/shard_map/reduce_scatter | solution.py:187
  311.3 1.0 copy-start
  317.3 1.2 copy-start.1
  317.3 148.4 %copy-start.3 = (bf16[512,512]{1,0:T(8,128)(2,1)S(1)}, bf16[512,512]{1,0:T(8,128)(2,1)}, u32[]{:S(2)}) copy-start(bf16[512,512]{1,0:T(8,128)(2,1)} %copy-done.2) | copy-start | bytes 1572868
  465.9 1.3 copy-start.9
  465.9 1.3 copy-start.12
  477.5 10.8 %collective-permute-start = (bf16[64,512]{1,0:T(8,128)(2,1)S(1)}, bf16[64,512]{1,0:T(8,128)(2,1)S(1)}, u32[]{:S(2)}, u32[]{:S(2)}) collective-permute-start(bf16[64,512]{1,0:T(8,128)(2,1)S(1)} %bitcast.174), channel_id=1, source_target_pairs={{0,4},{4,8},{8,12},{12,16},{16,20},{20,24},{24,28},{28,32},{32,36}... | collective-permute-start | bytes 196616 | tf_op jit(solution)/shard_map/ppermute | solution.py:19
  489.2 7.0 %collective-permute-start.1 = (bf16[64,512]{1,0:T(8,128)(2,1)S(1)}, bf16[64,512]{1,0:T(8,128)(2,1)S(1)}, u32[]{:S(2)}, u32[]{:S(2)}) collective-permute-start(bf16[64,512]{1,0:T(8,128)(2,1)S(1)} %slice_bitcast_fusion.1), channel_id=1, source_target_pairs={{0,4},{4,8},{8,12},{12,16},{16,20},{20,24},{24,28},{28,32},{32,36}... | collective-permute-start | bytes 196616 | tf_op jit(solution)/shard_map/ppermute | solution.py:19
Sparse Core Ops, SparseCore 0:
  28.4 152.5 all-gather.2
  317.4 154.2 reduce-scatter.1
